TPU v7x, 256 devices: a whole 4x4x8 slice. The times are simulated.
256 devices in a mesh: gy: 8 (over y, x_hi), gx: 4 (over x_lo, core), wa: 8 (over z).
Axes of the slice: x: 4 (x_hi: 2, x_lo: 2; x = x_hi * 2 + x_lo), y: 4, z: 8, core: 2. Of those that a mesh axis runs over, the one named last changes fastest.
Arguments:
- tokens: bfloat16 [8, 64, 128, 3072], P('wa', 'gy', 'gx'), may hold values from -6 to 6
- mod_shift: float32 [8, 3072], P('wa'), may hold values from -3 to 3
- mod_scale: float32 [8, 3072], P('wa'), may hold values from -0.9 to 3.9
- qkv_weight: bfloat16 [3072, 4608], P(None, ('gx', 'wa')), may hold values from -0.14433757 to 0.14433757
- block_codes: int32 [8, 16, 9], P('gy', 'gx'), may hold values from 0 to 8, as said below
- block_counts: int32 [8, 16], P('gy', 'gx'), may hold values from 1 to 9, as said below
- valid_tokens: int32 [8, 16], replicated, may hold values from 1 to 64
Outputs:
- attended: bfloat16 [8, 64, 128, 1536], P('wa', 'gy', 'gx')
Inputs may be any that keep to these rules, and one draw needn't show every extreme that they name: `block_codes`: the 9 codes of a block's list are distinct, the first is 4 (the block itself), and the first block_counts entries name blocks inside the grid. `block_counts`: A count never exceeds the number of blocks of the 3 x 3 neighbourhood that lie inside the grid.
All inputs are finite; a program needn't handle non-finite values.
Results may differ from a plain program's by a relative error of at most 0.007.
Values may be sent and summed in bfloat16 or wider, within the bound.
No kernel may reach another device: no remote copies, remote signals or barrier semaphores. Data moves between devices by JAX's collectives and lax.ppermute only.
A program may use at most 128 MiB of HBM per device.

v0:
```python
import math
import jax
import jax.numpy as jnp
from jax import lax
from jax.sharding import PartitionSpec as P

D = 3072
HEADS = 12
HD = 128
BLK = 8
NBR = 9


def extended_2(array, sides, width):
    for axis, dim in sides:
        size, length = (lax.axis_size(axis), array.shape[dim])
        up = [(i, (i + 1) % size) for i in range(size - 1)]
        down = [(j, i) for i, j in up]
        last = lax.slice_in_dim(array, length - width, length, axis=dim)
        first = lax.slice_in_dim(array, 0, width, axis=dim)
        before = lax.ppermute(last, axis, up)
        after = lax.ppermute(first, axis, down)
        array = jnp.concatenate([before, array, after], axis=dim)
    return array


def normalize(rows, shift_row, scale_row):
    widened = rows.astype(jnp.float32)
    average = jnp.mean(widened, axis=-1, keepdims=True)
    centred = widened - average
    spread = jnp.mean(centred * centred, axis=-1, keepdims=True)
    return (centred * lax.rsqrt(spread + 1e-06) * (1.0 + scale_row) + shift_row).astype(
        jnp.bfloat16
    )


def to_blocks(field):
    height, breadth, channels = field.shape
    shaped = field.reshape(height // BLK, BLK, breadth // BLK, BLK, channels)
    return shaped.transpose(0, 2, 1, 3, 4).reshape(
        height // BLK, breadth // BLK, BLK * BLK, channels
    )


def from_blocks(blocks):
    block_rows, block_cols, cells, channels = blocks.shape
    shaped = blocks.reshape(block_rows, block_cols, BLK, BLK, channels)
    return shaped.transpose(0, 2, 1, 3, 4).reshape(block_rows * BLK, block_cols * BLK, channels)


def make_mask(counts, live_count):
    slot_ids = jnp.arange(NBR, dtype=jnp.int32)
    token_ids = jnp.arange(BLK * BLK, dtype=jnp.int32)
    used = slot_ids[:, None] < counts[..., None, None]
    return used & (token_ids < live_count[..., None])


def attend(queries, key_blocks, key_mask):
    number = queries.shape[0]
    query_heads = queries.reshape(number, BLK * BLK, HEADS, HD)
    key_value = key_blocks.reshape(number, NBR * BLK * BLK, 2, HEADS, HD)
    scores = jnp.einsum(
        "nqhd,nkhd->nhqk", query_heads, key_value[:, :, 0], preferred_element_type=jnp.float32
    ) * (1.0 / math.sqrt(HD))
    scores = jnp.where(key_mask[:, None, None, :], scores, -jnp.inf)
    highest = jnp.max(scores, axis=-1, keepdims=True)
    exponent = jnp.exp(scores - highest)
    probs = (exponent / jnp.sum(exponent, axis=-1, keepdims=True)).astype(jnp.bfloat16)
    blended = jnp.einsum(
        "nhqk,nkhd->nqhd", probs, key_value[:, :, 1], preferred_element_type=jnp.float32
    )
    return blended.astype(jnp.bfloat16).reshape(number, BLK * BLK, HEADS * HD)


def body(tokens, mod_shift, mod_scale, qkv_weight, block_codes, block_counts, valid_tokens):
    tile_rows = tokens.shape[1]
    tile_cols = tokens.shape[2]
    width = HEADS * HD
    weight_block = lax.all_gather(qkv_weight, "wa", axis=1, tiled=True)
    flat_rows = normalize(tokens[0], mod_shift[0], mod_scale[0]).reshape(tile_rows * tile_cols, D)
    row_group = lax.all_gather(flat_rows, "gx", axis=0, tiled=True)
    partial = jnp.dot(row_group, weight_block, preferred_element_type=jnp.float32).astype(
        jnp.bfloat16
    )
    qkv = lax.all_to_all(partial, "gx", 0, 1, tiled=True)
    qkv_grid = qkv.reshape(tile_rows, tile_cols, 3 * width)
    extended = extended_2(qkv_grid[:, :, width:], (("gy", 0), ("gx", 1)), BLK)
    block_rows = tile_rows // BLK
    block_cols = tile_cols // BLK
    queries = to_blocks(qkv_grid[:, :, :width])
    key_blocks = to_blocks(extended)
    row_ids = jnp.arange(block_rows, dtype=jnp.int32)[:, None, None]
    col_ids = jnp.arange(block_cols, dtype=jnp.int32)[None, :, None]
    row_step = block_codes // 3 - 1
    col_step = block_codes % 3 - 1
    picked = key_blocks[row_ids + 1 + row_step, col_ids + 1 + col_step]
    global_row = jnp.clip(
        lax.axis_index("gy") * block_rows + row_ids + row_step, 0, valid_tokens.shape[0] - 1
    )
    global_col = jnp.clip(
        lax.axis_index("gx") * block_cols + col_ids + col_step, 0, valid_tokens.shape[1] - 1
    )
    live_count = valid_tokens[global_row, global_col]
    key_mask = make_mask(block_counts, live_count)
    number = block_rows * block_cols
    result = attend(
        queries.reshape(number, BLK * BLK, width),
        picked.reshape(number, NBR, BLK * BLK, 2 * width),
        key_mask.reshape(number, NBR * BLK * BLK),
    )
    return from_blocks(result.reshape(block_rows, block_cols, BLK * BLK, width))[None]


def solution(mesh):
    return jax.shard_map(
        body,
        mesh=mesh,
        in_specs=(
            P("wa", "gy", "gx", None),
            P("wa", None),
            P("wa", None),
            P(None, ("gx", "wa")),
            P("gy", "gx", None),
            P("gy", "gx"),
            P(),
        ),
        out_specs=P("wa", "gy", "gx", None),
        check_vma=False,
    )
```

profile of v0, /device:TPU:25, one launch (start us, length us, event | category | flops | bytes accessed | tf_op | source)
XLA Modules:
  0.0 396.4 jit_solution(5357344674858160736)
XLA Ops:
  11.1 3.3 fusion.12
  15.2 69.0 %all-gather.3.cloned.1.call-done = bf16[1024,3072]{1,0:T(8,128)(2,1)} async-done(((bf16[256,3072]{1,0:T(8,128)(2,1)}), bf16[1024,3072]{1,0:T(8,128)(2,1)}) %all-gather.3.cloned.1.call-update) | async-done | bytes 6291472 | tf_op jit(solution)/shard_map/all_gather | solution.py:81
  84.2 83.9 %all-gather.5.cloned.1.call-done = bf16[3072,1152]{0,1:T(8,128)(2,1)} async-done(((bf16[3072,144]{0,1:T(8,128)(2,1)}), bf16[3072,1152]{0,1:T(8,128)(2,1)}) %all-gather.5.cloned.1.call-update) | async-done | bytes 7077904 | tf_op jit(solution)/shard_map/all_gather | solution.py:79
  168.2 12.5 %convolution_convert_fusion = bf16[1024,1152]{1,0:T(8,128)(2,1)S(1)} fusion(bf16[1024,3072]{1,0:T(8,128)(2,1)} %all-gather.3.cloned.1.call-done, bf16[3072,1152]{0,1:T(8,128)(2,1)} %all-gather.5.cloned.1.call-done), kind=kOutput, calls=%fused_computation.16 | convolution fusion | flops 7248936960 | bytes 15728640 | tf_op jit(solution)/shard_map/dot_general | solution.py:82
  180.7 30.8 %all_to_all.16 = bf16[4,256,1152]{2,1,0:T(8,128)(2,1)S(1)} all-to-all(bf16[4,256,1152]{2,1,0:T(8,128)(2,1)S(1)} %bitcast.72), channel_id=1, replica_groups=mesh['gy'=8,'gx'=4,'wa'=8] {'gx'}, dimensions={0} | all-to-all | bytes 4718592 | tf_op jit(solution)/shard_map/all_to_all | solution.py:85
  213.3 2.4 reshape.129
  217.3 4.8 %collective-permute-start.1 = (bf16[8,32,3072]{2,1,0:T(8,128)(2,1)S(1)}, bf16[8,32,3072]{2,1,0:T(8,128)(2,1)S(1)}, u32[]{:S(2)}, u32[]{:S(2)}) collective-permute-start(bf16[8,32,3072]{2,1,0:T(8,128)(2,1)S(1)} %slice.31), channel_id=1, source_target_pairs={{32,0},{64,32},{96,64},{128,96},{160,128},{192,160},{224,192},{33,... | collective-permute-start | bytes 4718600 | tf_op jit(solution)/shard_map/ppermute | solution.py:22
  224.3 31.3 %collective-permute-done.1 = bf16[8,32,3072]{2,1,0:T(8,128)(2,1)S(1)} collective-permute-done((bf16[8,32,3072]{2,1,0:T(8,128)(2,1)S(1)}, bf16[8,32,3072]{2,1,0:T(8,128)(2,1)S(1)}, u32[]{:S(2)}, u32[]{:S(2)}) %collective-permute-start.1) | collective-permute-done | bytes 1572896 | tf_op jit(solution)/shard_map/ppermute | solution.py:22
  255.6 34.1 %collective-permute-done = bf16[8,32,3072]{2,1,0:T(8,128)(2,1)} collective-permute-done((bf16[8,32,3072]{2,1,0:T(8,128)(2,1)S(1)}, bf16[8,32,3072]{2,1,0:T(8,128)(2,1)}, u32[]{:S(2)}, u32[]{:S(2)}) %collective-permute-start) | collective-permute-done | bytes 1572896 | tf_op jit(solution)/shard_map/ppermute | solution.py:21
  289.7 2.8 pad_maximum_fusion.3
  292.4 4.3 %collective-permute-start.2 = (bf16[24,8,3072]{2,1,0:T(8,128)(2,1)}, bf16[24,8,3072]{2,1,0:T(8,128)(2,1)}, u32[]{:S(2)}, u32[]{:S(2)}) collective-permute-start(bf16[24,8,3072]{2,1,0:T(8,128)(2,1)} %get-tuple-element.7), channel_id=1, source_target_pairs={{0,8},{8,16},{16,24},{1,9},{9,17},{17,25},{2,10},{10,18},{18,26},{... | collective-permute-start | bytes 3538952 | tf_op jit(solution)/shard_map/ppermute | solution.py:21
  296.7 2.1 collective-permute-start.3
  300.4 2.1 copy_bitcast_fusion.10
  302.5 2.4 reshape_reshape_reshape.6
  304.9 5.2 %collective-permute-done.2 = bf16[24,8,3072]{2,1,0:T(8,128)(2,1)} collective-permute-done((bf16[24,8,3072]{2,1,0:T(8,128)(2,1)}, bf16[24,8,3072]{2,1,0:T(8,128)(2,1)}, u32[]{:S(2)}, u32[]{:S(2)}) %collective-permute-start.2) | collective-permute-done | bytes 1179680 | tf_op jit(solution)/shard_map/ppermute | solution.py:21
  310.1 4.4 %collective-permute-done.3 = bf16[24,8,3072]{2,1,0:T(8,128)(2,1)} collective-permute-done((bf16[24,8,3072]{2,1,0:T(8,128)(2,1)}, bf16[24,8,3072]{2,1,0:T(8,128)(2,1)}, u32[]{:S(2)}, u32[]{:S(2)}) %collective-permute-start.3) | collective-permute-done | bytes 1179680 | tf_op jit(solution)/shard_map/ppermute | solution.py:22
  314.5 3.3 pad_maximum_fusion
  317.8 3.7 copy.46
  321.6 10.6 %gather_fusion = bf16[36,64,3072]{2,1,0:T(8,128)(2,1)} fusion(bf16[3,6,64,3072]{3,2,1,0:T(8,128)(2,1)} %bitcast.69, s32[36]{0:T(128)S(1)} %reshape.136), kind=kCustom, calls=%fused_computation | custom fusion | bytes 28311840 | tf_op jit(solution)/shard_map/gather | solution.py:96
  332.1 25.4 %reshape_reshape.3 = bf16[4,576,2,12,128]{4,3,2,1,0:T(8,128)(2,1)} reshape(bf16[36,64,3072]{2,1,0:T(8,128)(2,1)} %gather_fusion) | data formatting | bytes 28311552 | tf_op jit(solution)/shard_map/reshape;reshape | solution.py:61
  357.5 12.5 %fusion.30 = (bf16[4,576,1,12,128]{4,3,2,1,0:T(8,128)(2,1)S(1)}, bf16[4,576,1,12,128]{4,3,2,1,0:T(8,128)(2,1)}) fusion(bf16[4,576,2,12,128]{4,3,2,1,0:T(8,128)(2,1)} %reshape_reshape.3), kind=kLoop, calls=%fused_computation.70 | loop fusion | bytes 28311552 | tf_op jit(solution)/shard_map/slice | solution.py:63
  370.1 3.4 fusion.2
  373.5 4.4 %fusion.31 = (f32[4,12,64]{2,1,0:T(8,128)S(1)}, f32[4,12,64,576]{3,2,1,0:T(8,128)}) fusion(f32[4,12,64,576]{3,2,1,0:T(8,128)S(1)} %fusion.2, pred[4,576]{1,0:T(4,128)(4,1)S(1)} %compare_and_fusion), kind=kOutput, calls=%fused_computation.71 | output fusion | flops 10617407 | bytes 14170368 | tf_op jit(solution)/shard_map/sub | solution.py:67
  377.9 9.6 %fusion.14 = bf16[4,64,12,128]{3,1,2,0:T(8,128)(2,1)S(1)} fusion(bf16[4,576,1,12,128]{4,3,2,1,0:T(8,128)(2,1)} %get-tuple-element.6, f32[4,12,64,576]{3,2,1,0:T(8,128)} %get-tuple-element.14, f32[4,12,64]{2,1,0:T(8,128)S(1)} %get-tuple-element.13), kind=kOutput, calls=%fused_computation.27 | convolution fusion | flops 456916992 | bytes 14954496 | tf_op jit(solution)/shard_map/nhqk,nkhd->nqhd/dot_general | solution.py:69
  (45 shorter events, 14.5 us)
Async XLA Ops:
  6.5 292.4 %copy-start = (s32[8,16]{1,0:T(8,128)S(1)}, s32[8,16]{1,0:T(8,128)}, u32[]{:S(2)}) copy-start(s32[8,16]{1,0:T(8,128)} %param.13) | copy-start | bytes 1540
  6.5 77.7 %all-gather.3.cloned.1.call-start = ((), (), s32[]{:S(2)}) async-start(), calls=%async_computation.1 | async-start | bytes 7864320 | tf_op jit(solution)/shard_map/all_gather | solution.py:81
  14.5 153.7 %all-gather.5.cloned.1.call-start = ((), (), s32[]{:S(2)}) async-start(), calls=%async_computation.2 | async-start | bytes 7962624 | tf_op jit(solution)/shard_map/all_gather | solution.py:79
  213.3 10.9 %copy-start.3 = (s32[1,4,9]{2,1,0:T(4,128)S(1)}, s32[1,4,9]{2,1,0:T(4,128)}, u32[]{:S(2)}) copy-start(s32[1,4,9]{2,1,0:T(4,128)} %param.11) | copy-start | bytes 436
  217.3 82.7 %copy-start.4 = (s32[1,4]{1,0:T(1,128)S(1)}, s32[1,4]{1,0:T(1,128)}, u32[]{:S(2)}) copy-start(s32[1,4]{1,0:T(1,128)} %param.12) | copy-start | bytes 52
  217.3 38.3 %collective-permute-start.1 = (bf16[8,32,3072]{2,1,0:T(8,128)(2,1)S(1)}, bf16[8,32,3072]{2,1,0:T(8,128)(2,1)S(1)}, u32[]{:S(2)}, u32[]{:S(2)}) collective-permute-start(bf16[8,32,3072]{2,1,0:T(8,128)(2,1)S(1)} %slice.31), channel_id=1, source_target_pairs={{32,0},{64,32},{96,64},{128,96},{160,128},{192,160},{224,192},{33,... | collective-permute-start | bytes 4718600 | tf_op jit(solution)/shard_map/ppermute | solution.py:22
  222.1 67.6 %collective-permute-start = (bf16[8,32,3072]{2,1,0:T(8,128)(2,1)S(1)}, bf16[8,32,3072]{2,1,0:T(8,128)(2,1)}, u32[]{:S(2)}, u32[]{:S(2)}) collective-permute-start(bf16[8,32,3072]{2,1,0:T(8,128)(2,1)S(1)} %slice.31), channel_id=1, source_target_pairs={{0,32},{32,64},{64,96},{96,128},{128,160},{160,192},{192,224},{1,3... | collective-permute-start | bytes 4718600 | tf_op jit(solution)/shard_map/ppermute | solution.py:21
  292.4 17.7 %collective-permute-start.2 = (bf16[24,8,3072]{2,1,0:T(8,128)(2,1)}, bf16[24,8,3072]{2,1,0:T(8,128)(2,1)}, u32[]{:S(2)}, u32[]{:S(2)}) collective-permute-start(bf16[24,8,3072]{2,1,0:T(8,128)(2,1)} %get-tuple-element.7), channel_id=1, source_target_pairs={{0,8},{8,16},{16,24},{1,9},{9,17},{17,25},{2,10},{10,18},{18,26},{... | collective-permute-start | bytes 3538952 | tf_op jit(solution)/shard_map/ppermute | solution.py:21
  296.7 17.8 %collective-permute-start.3 = (bf16[24,8,3072]{2,1,0:T(8,128)(2,1)}, bf16[24,8,3072]{2,1,0:T(8,128)(2,1)}, u32[]{:S(2)}, u32[]{:S(2)}) collective-permute-start(bf16[24,8,3072]{2,1,0:T(8,128)(2,1)} %get-tuple-element.8), channel_id=1, source_target_pairs={{8,0},{16,8},{24,16},{9,1},{17,9},{25,17},{10,2},{18,10},{26,18},{... | collective-permute-start | bytes 3538952 | tf_op jit(solution)/shard_map/ppermute | solution.py:22
  357.5 12.5 %copy-start.2 = (bf16[4,64,12,128]{3,2,1,0:T(8,128)(2,1)S(1)}, bf16[4,64,12,128]{3,2,1,0:T(8,128)(2,1)}, u32[]{:S(2)}) copy-start(bf16[4,64,12,128]{3,2,1,0:T(8,128)(2,1)} %reshape_reshape_reshape.6) | copy-start | bytes 2359300
  377.9 11.6 %copy-start.1 = (s32[8,16]{1,0:T(8,128)S(1)}, s32[8,16]{1,0:T(8,128)}, u32[]{:S(2)}) copy-start(s32[8,16]{1,0:T(8,128)} %param.13) | copy-start | bytes 1540
Sparse Core Ops, SparseCore 0:
  14.6 69.5 all-gather.2
  86.0 82.0 all-gather.4
where the time goes:
time: 398 us; the launch traced here: 396 us
  waiting for transfers between devices  229 us (58%)
  local copies, waits for them, and re-layouts  66.2 us (17%)
  blocking collectives  30.8 us (8%)
  matrix products  25.5 us (6%)
  other arithmetic  18.4 us (5%)
  between operations  13.6 us (3%)
  starting transfers between devices  13.3 us (3%)
    all_gather x1, waiting for transfers between devices, body(): weight_block = lax.all_gather(qkv_weight, 'wa', axis=1, tiled=True)  83.9 us
    all_gather x1, waiting for transfers between devices, body(): row_group = lax.all_gather(flat_rows, 'gx', axis=0, tiled=True)  69 us
    ppermute x2, waiting for transfers between devices, extended_2(): before = lax.ppermute(last, axis, up)  39.3 us
    ppermute x2, waiting for transfers between devices, extended_2(): after = lax.ppermute(first, axis, down)  35.7 us
    all_to_all x1, blocking collectives, body(): qkv = lax.all_to_all(partial, 'gx', 0, 1, tiled=True)  30.8 us
    another operation x1, local copies, waits for them, and re-layouts, attend(): key_value = key_blocks.reshape(number, NBR * BLK * BLK, 2, HEADS, HD)  25.4 us
    slice x1, local copies, waits for them, and re-layouts, attend(): key_value[:, :, 0]  12.5 us
    dot_general x1, matrix products, body(): jnp.dot(row_group, weight_block, preferred_element_type=jnp.float32)  12.5 us
  transfers between devices with their start and end apart: 6, of which 6 were waited for; matrix products, arithmetic and copies ran while one was open for 2% of the time, Pallas kernels for 0%

commit v1 on v0

--- a/solution.py
+++ b/solution.py
@@ -76,7 +76,26 @@
     tile_rows = tokens.shape[1]
     tile_cols = tokens.shape[2]
     width = HEADS * HD
-    weight_block = lax.all_gather(qkv_weight, "wa", axis=1, tiled=True)
+    a_next, v1, all_rows = (lax.psum(1, axis_name="wa"), lax.axis_index("wa"), qkv_weight.shape[1])
+    so_far_all = [idx * a_next if num == 1 else idx for num, idx in enumerate(qkv_weight.shape)]
+    weight_block = lax.dynamic_update_slice_in_dim(
+        jnp.zeros(so_far_all, qkv_weight.dtype), qkv_weight, v1 * all_rows, axis=1
+    )
+    z_new = newest = qkv_weight
+    for to_i in tuple(range(1, a_next // 2 + 1)):
+        z_new = lax.ppermute(
+            z_new, axis_name="wa", perm=[(num, (num + 1) % a_next) for num in range(a_next)]
+        )
+        weight_block = lax.dynamic_update_slice_in_dim(
+            weight_block, z_new, (v1 - to_i) % a_next * all_rows, axis=1
+        )
+        if 2 * to_i < a_next:
+            newest = lax.ppermute(
+                newest, axis_name="wa", perm=[(num, (num - 1) % a_next) for num in range(a_next)]
+            )
+            weight_block = lax.dynamic_update_slice_in_dim(
+                weight_block, newest, (v1 + to_i) % a_next * all_rows, axis=1
+            )
     flat_rows = normalize(tokens[0], mod_shift[0], mod_scale[0]).reshape(tile_rows * tile_cols, D)
     row_group = lax.all_gather(flat_rows, "gx", axis=0, tiled=True)
     partial = jnp.dot(row_group, weight_block, preferred_element_type=jnp.float32).astype(

time: 398 us -> 334 us (0.84)
  waiting for transfers between devices: 229 us -> 138 us
  local copies, waits for them, and re-layouts: 66.2 us -> 79 us
  starting transfers between devices: 13.3 us -> 24.1 us
    all_gather x1 -> x0, waiting for transfers between devices: 83.9 us -> none  [body(): weight_block = lax.all_gather(qkv_weight, 'wa', axis=1, tiled=True)]
    all_gather x1, waiting for transfers between devices: 69 us -> 0.01 us  [body(): row_group = lax.all_gather(flat_rows, 'gx', axis=0, tiled=True)]
    ppermute x0 -> x7, waiting for transfers between devices: none -> 63.2 us  [the longest x4 62.9 us: body(): lax.ppermute(z_new, axis_name='wa', perm=[(num, (num + 1) % a_next) for n...]
    ppermute x0 -> x7, starting transfers between devices: none -> 11.1 us  [the longest x3 9.4 us: body(): lax.ppermute(newest, axis_name='wa', perm=[(num, (num - 1) % a_next) for...]
    dynamic_update_slice x0 -> x8, local copies, waits for them, and re-layouts: none -> 9.07 us  [the longest x4 5.12 us: body(): lax.dynamic_update_slice_in_dim(weight_block, z_new, (v1 - to_i) % a_next...]
  transfers between devices with their start and end apart: 6 -> 12, of which waited for: 6 -> 9; matrix products, arithmetic and copies ran while one was open for 2% -> 6% of each run, Pallas kernels for 0% -> 0%
where the time goes in v1:
time: 334 us; the launch traced here: 333 us
  waiting for transfers between devices  138 us (41%)
  local copies, waits for them, and re-layouts  79 us (24%)
  blocking collectives  33.8 us (10%)
  matrix products  25.5 us (8%)
  starting transfers between devices  24.1 us (7%)
  other arithmetic  18.5 us (6%)
  between operations  13.6 us (4%)
    ppermute x4, waiting for transfers between devices, body(): lax.ppermute(z_new, axis_name='wa', perm=[(num, (num + 1) % a_next) for n...  62.9 us
    ppermute x2, waiting for transfers between devices, extended_2(): before = lax.ppermute(last, axis, up)  39.3 us
    ppermute x2, waiting for transfers between devices, extended_2(): after = lax.ppermute(first, axis, down)  35.7 us
    all_to_all x1, blocking collectives, body(): qkv = lax.all_to_all(partial, 'gx', 0, 1, tiled=True)  33.8 us
    another operation x1, local copies, waits for them, and re-layouts, attend(): key_value = key_blocks.reshape(number, NBR * BLK * BLK, 2, HEADS, HD)  25.4 us
    slice x1, local copies, waits for them, and re-layouts, attend(): key_value[:, :, 0]  12.5 us
    dot_general x1, matrix products, body(): jnp.dot(row_group, weight_block, preferred_element_type=jnp.float32)  12.5 us
    gather x1, local copies, waits for them, and re-layouts, body(): picked = key_blocks[row_ids + 1 + row_step, col_ids + 1 + col_step]  10.5 us
  transfers between devices with their start and end apart: 12, of which 9 were waited for; matrix products, arithmetic and copies ran while one was open for 6% of the time, Pallas kernels for 0%

profile of v1, /device:TPU:25, one launch (start us, length us, event | category | flops | bytes accessed | tf_op | source)
XLA Modules:
  0.0 332.8 jit_solution(14335047027872870338)
XLA Ops:
  11.2 3.3 %fusion.12 = bf16[256,3072]{1,0:T(8,128)(2,1)} fusion(bf16[1,8,32,3072]{3,2,1,0:T(8,128)(2,1)} %param.7, f32[3072]{0:T(1024)} %bitcast.74, f32[3072]{0:T(1024)S(1)} %bitcast.73, f32[256]{0:T(256)S(1)} %rsqrt.12, f32[256]{0:T(256)S(1)} %div.23), kind=kLoop, calls=%fused_computation.24 | loop fusion | flops 4718592 | bytes 3172352 | tf_op jit(solution)/shard_map/convert_element_type | solution.py:32
  16.3 4.0 %collective-permute-start.1 = (bf16[3072,144]{0,1:T(8,128)(2,1)S(1)}, bf16[3072,144]{0,1:T(8,128)(2,1)S(1)}, u32[]{:S(2)}, u32[]{:S(2)}) collective-permute-start(bf16[3072,144]{0,1:T(8,128)(2,1)S(1)} %copy-done.3), channel_id=1, source_target_pairs={{0,7},{1,0},{2,1},{3,2},{4,3},{5,4},{6,5},{7,6},{8,15},{9,8},{10,9... | collective-permute-start | bytes 2654216 | tf_op jit(solution)/shard_map/ppermute | solution.py:93
  20.3 19.4 %collective-permute-done = bf16[3072,144]{0,1:T(8,128)(2,1)} collective-permute-done((bf16[3072,144]{0,1:T(8,128)(2,1)S(1)}, bf16[3072,144]{0,1:T(8,128)(2,1)}, u32[]{:S(2)}, u32[]{:S(2)}) %collective-permute-start) | collective-permute-done | bytes 884768 | tf_op jit(solution)/shard_map/ppermute | solution.py:86
  42.3 3.8 %broadcast_in_dim.36 = bf16[3072,1152]{0,1:T(8,128)(2,1)} broadcast(bf16[]{:T(256)} %constant.96.clone.1), dimensions={} | broadcast | bytes 7077890 | tf_op jit(solution)/shard_map/broadcast_in_dim | solution.py:82
  47.1 13.9 %collective-permute-done.2 = bf16[3072,144]{0,1:T(8,128)(2,1)S(1)} collective-permute-done((bf16[3072,144]{0,1:T(8,128)(2,1)}, bf16[3072,144]{0,1:T(8,128)(2,1)S(1)}, u32[]{:S(2)}, u32[]{:S(2)}) %collective-permute-start.2) | collective-permute-done | bytes 884768 | tf_op jit(solution)/shard_map/ppermute | solution.py:86
  67.9 13.4 %collective-permute-done.4 = bf16[3072,144]{0,1:T(8,128)(2,1)S(1)} collective-permute-done((bf16[3072,144]{0,1:T(8,128)(2,1)S(1)}, bf16[3072,144]{0,1:T(8,128)(2,1)S(1)}, u32[]{:S(2)}, u32[]{:S(2)}) %collective-permute-start.4) | collective-permute-done | bytes 884768 | tf_op jit(solution)/shard_map/ppermute | solution.py:86
  84.6 16.2 %collective-permute-done.6 = bf16[3072,144]{0,1:T(8,128)(2,1)S(1)} collective-permute-done((bf16[3072,144]{0,1:T(8,128)(2,1)S(1)}, bf16[3072,144]{0,1:T(8,128)(2,1)S(1)}, u32[]{:S(2)}, u32[]{:S(2)}) %collective-permute-start.6) | collective-permute-done | bytes 884768 | tf_op jit(solution)/shard_map/ppermute | solution.py:86
  101.8 12.5 %convolution_convert_fusion = bf16[1024,1152]{1,0:T(8,128)(2,1)S(1)} fusion(bf16[1024,3072]{1,0:T(8,128)(2,1)} %all-gather.2.cloned.1.call-done, bf16[3072,1152]{0,1:T(8,128)(2,1)} %constant_dynamic-update-slice_fusion), kind=kOutput, calls=%fused_computation.16 | convolution fusion | flops 7248936960 | bytes 15728640 | tf_op jit(solution)/shard_map/dot_general | solution.py:101
  114.3 33.8 %all_to_all.16 = bf16[4,256,1152]{2,1,0:T(8,128)(2,1)S(1)} all-to-all(bf16[4,256,1152]{2,1,0:T(8,128)(2,1)S(1)} %bitcast.72), channel_id=1, replica_groups=mesh['gy'=8,'gx'=4,'wa'=8] {'gx'}, dimensions={0} | all-to-all | bytes 4718592 | tf_op jit(solution)/shard_map/all_to_all | solution.py:104
  153.9 4.8 %collective-permute-start.8 = (bf16[8,32,3072]{2,1,0:T(8,128)(2,1)S(1)}, bf16[8,32,3072]{2,1,0:T(8,128)(2,1)S(1)}, u32[]{:S(2)}, u32[]{:S(2)}) collective-permute-start(bf16[8,32,3072]{2,1,0:T(8,128)(2,1)S(1)} %slice.31), channel_id=1, source_target_pairs={{32,0},{64,32},{96,64},{128,96},{160,128},{192,160},{224,192},{33,... | collective-permute-start | bytes 4718600 | tf_op jit(solution)/shard_map/ppermute | solution.py:22
  160.9 31.3 %collective-permute-done.8 = bf16[8,32,3072]{2,1,0:T(8,128)(2,1)S(1)} collective-permute-done((bf16[8,32,3072]{2,1,0:T(8,128)(2,1)S(1)}, bf16[8,32,3072]{2,1,0:T(8,128)(2,1)S(1)}, u32[]{:S(2)}, u32[]{:S(2)}) %collective-permute-start.8) | collective-permute-done | bytes 1572896 | tf_op jit(solution)/shard_map/ppermute | solution.py:22
  192.2 34.0 %collective-permute-done.7 = bf16[8,32,3072]{2,1,0:T(8,128)(2,1)} collective-permute-done((bf16[8,32,3072]{2,1,0:T(8,128)(2,1)S(1)}, bf16[8,32,3072]{2,1,0:T(8,128)(2,1)}, u32[]{:S(2)}, u32[]{:S(2)}) %collective-permute-start.7) | collective-permute-done | bytes 1572896 | tf_op jit(solution)/shard_map/ppermute | solution.py:21
  226.2 2.8 pad_maximum_fusion.3
  229.0 4.1 %collective-permute-start.9 = (bf16[24,8,3072]{2,1,0:T(8,128)(2,1)}, bf16[24,8,3072]{2,1,0:T(8,128)(2,1)}, u32[]{:S(2)}, u32[]{:S(2)}) collective-permute-start(bf16[24,8,3072]{2,1,0:T(8,128)(2,1)} %get-tuple-element.7), channel_id=1, source_target_pairs={{0,8},{8,16},{16,24},{1,9},{9,17},{17,25},{2,10},{10,18},{18,26},{... | collective-permute-start | bytes 3538952 | tf_op jit(solution)/shard_map/ppermute | solution.py:21
  241.2 5.3 %collective-permute-done.9 = bf16[24,8,3072]{2,1,0:T(8,128)(2,1)} collective-permute-done((bf16[24,8,3072]{2,1,0:T(8,128)(2,1)}, bf16[24,8,3072]{2,1,0:T(8,128)(2,1)}, u32[]{:S(2)}, u32[]{:S(2)}) %collective-permute-start.9) | collective-permute-done | bytes 1179680 | tf_op jit(solution)/shard_map/ppermute | solution.py:21
  246.5 4.4 %collective-permute-done.10 = bf16[24,8,3072]{2,1,0:T(8,128)(2,1)} collective-permute-done((bf16[24,8,3072]{2,1,0:T(8,128)(2,1)}, bf16[24,8,3072]{2,1,0:T(8,128)(2,1)}, u32[]{:S(2)}, u32[]{:S(2)}) %collective-permute-start.10) | collective-permute-done | bytes 1179680 | tf_op jit(solution)/shard_map/ppermute | solution.py:22
  250.9 3.3 pad_maximum_fusion
  254.2 3.7 %copy.46 = bf16[3,8,6,8,3072]{4,3,1,2,0:T(8,128)(2,1)} copy(bf16[3,8,6,8,3072]{4,3,2,1,0:T(8,128)(2,1)S(1)} %bitcast.70) | data formatting | bytes 14155776 | tf_op jit(solution)/shard_map/reshape | solution.py:39
  258.0 10.5 %gather_fusion = bf16[36,64,3072]{2,1,0:T(8,128)(2,1)} fusion(bf16[3,6,64,3072]{3,2,1,0:T(8,128)(2,1)} %bitcast.69, s32[36]{0:T(128)S(1)} %reshape.136), kind=kCustom, calls=%fused_computation | custom fusion | bytes 28311840 | tf_op jit(solution)/shard_map/gather | solution.py:115
  268.5 25.4 %reshape_reshape.3 = bf16[4,576,2,12,128]{4,3,2,1,0:T(8,128)(2,1)} reshape(bf16[36,64,3072]{2,1,0:T(8,128)(2,1)} %gather_fusion) | data formatting | bytes 28311552 | tf_op jit(solution)/shard_map/reshape;reshape | solution.py:61
  293.9 12.5 %fusion.30 = (bf16[4,576,1,12,128]{4,3,2,1,0:T(8,128)(2,1)S(1)}, bf16[4,576,1,12,128]{4,3,2,1,0:T(8,128)(2,1)}) fusion(bf16[4,576,2,12,128]{4,3,2,1,0:T(8,128)(2,1)} %reshape_reshape.3), kind=kLoop, calls=%fused_computation.78 | loop fusion | bytes 28311552 | tf_op jit(solution)/shard_map/slice | solution.py:63
  306.5 3.4 %fusion.2 = f32[4,12,64,576]{3,2,1,0:T(8,128)S(1)} fusion(bf16[4,576,1,12,128]{4,3,2,1,0:T(8,128)(2,1)S(1)} %get-tuple-element.5, bf16[4,64,12,128]{3,2,1,0:T(8,128)(2,1)S(1)} %copy-done.2), kind=kOutput, calls=%fused_computation.10 | convolution fusion | flops 452984832 | bytes 14942208 | tf_op jit(solution)/shard_map/nqhd,nkhd->nhqk/dot_general | solution.py:62
  309.9 4.4 %fusion.31 = (f32[4,12,64]{2,1,0:T(8,128)S(1)}, f32[4,12,64,576]{3,2,1,0:T(8,128)}) fusion(f32[4,12,64,576]{3,2,1,0:T(8,128)S(1)} %fusion.2, pred[4,576]{1,0:T(4,128)(4,1)S(1)} %compare_and_fusion), kind=kOutput, calls=%fused_computation.79 | output fusion | flops 10617407 | bytes 14170368 | tf_op jit(solution)/shard_map/sub | solution.py:67
  314.3 9.6 %fusion.14 = bf16[4,64,12,128]{3,1,2,0:T(8,128)(2,1)S(1)} fusion(bf16[4,576,1,12,128]{4,3,2,1,0:T(8,128)(2,1)} %get-tuple-element.6, f32[4,12,64,576]{3,2,1,0:T(8,128)} %get-tuple-element.14, f32[4,12,64]{2,1,0:T(8,128)S(1)} %get-tuple-element.13), kind=kOutput, calls=%fused_computation.27 | convolution fusion | flops 456916992 | bytes 14954496 | tf_op jit(solution)/shard_map/nhqk,nkhd->nqhd/dot_general | solution.py:69
  (67 shorter events, 39.2 us)
Async XLA Ops:
  6.5 228.7 %copy-start = (s32[8,16]{1,0:T(8,128)S(1)}, s32[8,16]{1,0:T(8,128)}, u32[]{:S(2)}) copy-start(s32[8,16]{1,0:T(8,128)} %param.13) | copy-start | bytes 1540
  6.5 8.0 %copy-start.3 = (bf16[3072,144]{0,1:T(8,128)(2,1)S(1)}, bf16[3072,144]{0,1:T(8,128)(2,1)}, u32[]{:S(2)}) copy-start(bf16[3072,144]{0,1:T(8,128)(2,1)} %param.10) | copy-start | bytes 2654212
  6.5 95.2 %all-gather.2.cloned.1.call-start = ((), (), s32[]{:S(2)}) async-start(), calls=%async_computation.1 | async-start | bytes 7864320 | tf_op jit(solution)/shard_map/all_gather | solution.py:100
  14.5 25.1 %collective-permute-start = (bf16[3072,144]{0,1:T(8,128)(2,1)S(1)}, bf16[3072,144]{0,1:T(8,128)(2,1)}, u32[]{:S(2)}, u32[]{:S(2)}) collective-permute-start(bf16[3072,144]{0,1:T(8,128)(2,1)S(1)} %copy-done.3), channel_id=1, source_target_pairs={{0,1},{1,2},{2,3},{3,4},{4,5},{5,6},{6,7},{7,0},{8,9},{9,10},{10,1... | collective-permute-start | bytes 2654216 | tf_op jit(solution)/shard_map/ppermute | solution.py:86
  16.3 23.4 %collective-permute-start.1 = (bf16[3072,144]{0,1:T(8,128)(2,1)S(1)}, bf16[3072,144]{0,1:T(8,128)(2,1)S(1)}, u32[]{:S(2)}, u32[]{:S(2)}) collective-permute-start(bf16[3072,144]{0,1:T(8,128)(2,1)S(1)} %copy-done.3), channel_id=1, source_target_pairs={{0,7},{1,0},{2,1},{3,2},{4,3},{5,4},{6,5},{7,6},{8,15},{9,8},{10,9... | collective-permute-start | bytes 2654216 | tf_op jit(solution)/shard_map/ppermute | solution.py:93
  39.7 21.4 %collective-permute-start.2 = (bf16[3072,144]{0,1:T(8,128)(2,1)}, bf16[3072,144]{0,1:T(8,128)(2,1)S(1)}, u32[]{:S(2)}, u32[]{:S(2)}) collective-permute-start(bf16[3072,144]{0,1:T(8,128)(2,1)} %collective-permute-done), channel_id=1, source_target_pairs={{0,1},{1,2},{2,3},{3,4},{4,5},{5,6},{6,7},{7,0},{8,9},{9,10},{10,1... | collective-permute-start | bytes 2654216 | tf_op jit(solution)/shard_map/ppermute | solution.py:86
  39.7 24.6 %collective-permute-start.3 = (bf16[3072,144]{0,1:T(8,128)(2,1)S(1)}, bf16[3072,144]{0,1:T(8,128)(2,1)S(1)}, u32[]{:S(2)}, u32[]{:S(2)}) collective-permute-start(bf16[3072,144]{0,1:T(8,128)(2,1)S(1)} %collective-permute-done.1), channel_id=1, source_target_pairs={{0,7},{1,0},{2,1},{3,2},{4,3},{5,4},{6,5},{7,6},{8,15},{9,8},{10,9... | collective-permute-start | bytes 2654216 | tf_op jit(solution)/shard_map/ppermute | solution.py:93
  61.0 20.3 %collective-permute-start.4 = (bf16[3072,144]{0,1:T(8,128)(2,1)S(1)}, bf16[3072,144]{0,1:T(8,128)(2,1)S(1)}, u32[]{:S(2)}, u32[]{:S(2)}) collective-permute-start(bf16[3072,144]{0,1:T(8,128)(2,1)S(1)} %collective-permute-done.2), channel_id=1, source_target_pairs={{0,1},{1,2},{2,3},{3,4},{4,5},{5,6},{6,7},{7,0},{8,9},{9,10},{10,1... | collective-permute-start | bytes 2654216 | tf_op jit(solution)/shard_map/ppermute | solution.py:86
  64.2 19.4 %collective-permute-start.5 = (bf16[3072,144]{0,1:T(8,128)(2,1)S(1)}, bf16[3072,144]{0,1:T(8,128)(2,1)S(1)}, u32[]{:S(2)}, u32[]{:S(2)}) collective-permute-start(bf16[3072,144]{0,1:T(8,128)(2,1)S(1)} %collective-permute-done.3), channel_id=1, source_target_pairs={{0,7},{1,0},{2,1},{3,2},{4,3},{5,4},{6,5},{7,6},{8,15},{9,8},{10,9... | collective-permute-start | bytes 2654216 | tf_op jit(solution)/shard_map/ppermute | solution.py:93
  81.4 19.5 %collective-permute-start.6 = (bf16[3072,144]{0,1:T(8,128)(2,1)S(1)}, bf16[3072,144]{0,1:T(8,128)(2,1)S(1)}, u32[]{:S(2)}, u32[]{:S(2)}) collective-permute-start(bf16[3072,144]{0,1:T(8,128)(2,1)S(1)} %collective-permute-done.4), channel_id=1, source_target_pairs={{0,1},{1,2},{2,3},{3,4},{4,5},{5,6},{6,7},{7,0},{8,9},{9,10},{10,1... | collective-permute-start | bytes 2654216 | tf_op jit(solution)/shard_map/ppermute | solution.py:86
  148.1 12.7 %copy-start.4 = (s32[1,4,9]{2,1,0:T(4,128)S(1)}, s32[1,4,9]{2,1,0:T(4,128)}, u32[]{:S(2)}) copy-start(s32[1,4,9]{2,1,0:T(4,128)} %param.11) | copy-start | bytes 436
  152.3 84.0 %copy-start.5 = (s32[1,4]{1,0:T(1,128)S(1)}, s32[1,4]{1,0:T(1,128)}, u32[]{:S(2)}) copy-start(s32[1,4]{1,0:T(1,128)} %param.12) | copy-start | bytes 52
  153.9 38.3 %collective-permute-start.8 = (bf16[8,32,3072]{2,1,0:T(8,128)(2,1)S(1)}, bf16[8,32,3072]{2,1,0:T(8,128)(2,1)S(1)}, u32[]{:S(2)}, u32[]{:S(2)}) collective-permute-start(bf16[8,32,3072]{2,1,0:T(8,128)(2,1)S(1)} %slice.31), channel_id=1, source_target_pairs={{32,0},{64,32},{96,64},{128,96},{160,128},{192,160},{224,192},{33,... | collective-permute-start | bytes 4718600 | tf_op jit(solution)/shard_map/ppermute | solution.py:22
  158.6 67.5 %collective-permute-start.7 = (bf16[8,32,3072]{2,1,0:T(8,128)(2,1)S(1)}, bf16[8,32,3072]{2,1,0:T(8,128)(2,1)}, u32[]{:S(2)}, u32[]{:S(2)}) collective-permute-start(bf16[8,32,3072]{2,1,0:T(8,128)(2,1)S(1)} %slice.31), channel_id=1, source_target_pairs={{0,32},{32,64},{64,96},{96,128},{128,160},{160,192},{192,224},{1,3... | collective-permute-start | bytes 4718600 | tf_op jit(solution)/shard_map/ppermute | solution.py:21
  229.0 17.6 %collective-permute-start.9 = (bf16[24,8,3072]{2,1,0:T(8,128)(2,1)}, bf16[24,8,3072]{2,1,0:T(8,128)(2,1)}, u32[]{:S(2)}, u32[]{:S(2)}) collective-permute-start(bf16[24,8,3072]{2,1,0:T(8,128)(2,1)} %get-tuple-element.7), channel_id=1, source_target_pairs={{0,8},{8,16},{16,24},{1,9},{9,17},{17,25},{2,10},{10,18},{18,26},{... | collective-permute-start | bytes 3538952 | tf_op jit(solution)/shard_map/ppermute | solution.py:21
  233.1 17.8 %collective-permute-start.10 = (bf16[24,8,3072]{2,1,0:T(8,128)(2,1)}, bf16[24,8,3072]{2,1,0:T(8,128)(2,1)}, u32[]{:S(2)}, u32[]{:S(2)}) collective-permute-start(bf16[24,8,3072]{2,1,0:T(8,128)(2,1)} %get-tuple-element.8), channel_id=1, source_target_pairs={{8,0},{16,8},{24,16},{9,1},{17,9},{25,17},{10,2},{18,10},{26,18},{... | collective-permute-start | bytes 3538952 | tf_op jit(solution)/shard_map/ppermute | solution.py:22
  293.9 12.6 %copy-start.2 = (bf16[4,64,12,128]{3,2,1,0:T(8,128)(2,1)S(1)}, bf16[4,64,12,128]{3,2,1,0:T(8,128)(2,1)}, u32[]{:S(2)}) copy-start(bf16[4,64,12,128]{3,2,1,0:T(8,128)(2,1)} %reshape_reshape_reshape.6) | copy-start | bytes 2359300
  314.3 11.6 %copy-start.1 = (s32[8,16]{1,0:T(8,128)S(1)}, s32[8,16]{1,0:T(8,128)}, u32[]{:S(2)}) copy-start(s32[8,16]{1,0:T(8,128)} %param.13) | copy-start | bytes 1540
Sparse Core Ops, SparseCore 0:
  14.7 69.6 all-gather.1
